TPU v7x, 256 devices: a whole 4x4x8 slice. The times are simulated.
256 devices in a mesh: orient: 16 (over y, x_lo, core), strip: 16 (over x_hi, z).
Axes of the slice: x: 4 (x_hi: 2, x_lo: 2; x = x_hi * 2 + x_lo), y: 4, z: 8, core: 2. Of those that a mesh axis runs over, the one named last changes fastest.
Arguments:
- inflow_field: bfloat16 [32, 8, 128, 512], P('orient', None, 'strip'), may hold values from -6 to 6
- kernel_one: bfloat16 [32, 9, 8, 8], replicated, may hold values from -0.125 to 0.125
- kernel_two: bfloat16 [32, 9, 8, 8], replicated, may hold values from -0.125 to 0.125
- turbine_mask: int32 [128, 512], P('strip'), may hold values 0 or 1
- wind_sector: int32 [1], replicated, may hold values from 0 to 31
- wake_cotangent: bfloat16 [32, 8, 128, 512], P('orient', None, 'strip'), may hold values from -6 to 6
Outputs:
- wake_out: bfloat16 [32, 8, 128, 512], P('orient', None, 'strip')
- kernel_grad_one: float32 [32, 9, 8, 8], replicated
- kernel_grad_two: float32 [32, 9, 8, 8], replicated
Inputs may be any that keep to these rules, and one draw needn't show every extreme that they name: `wind_sector`: names one element of the group.
All inputs are finite; a program needn't handle non-finite values. No bound on the sum of `turbine_mask` on one device may be relied on, other than what follows from the above.
Results may differ from a plain program's by a relative error of at most 0.0051.
Values may be sent and summed in bfloat16 or wider, within the bound.
No kernel may reach another device: no remote copies, remote signals or barrier semaphores. Data moves between devices by JAX's collectives and lax.ppermute only.
A program may use at most 128 MiB of HBM per device.

v0:
```python
import math
import jax
import jax.numpy as jnp
from jax import lax
from jax.sharding import PartitionSpec as P

G = 32
OFFSETS = ((0, 0), (0, 1), (0, 2), (1, 0), (1, 1), (1, 2), (2, 0), (2, 1), (2, 2))


def with_halo(shard, sides, width):
    for axis, dim in sides:
        count, length = (lax.axis_size(axis), shard.shape[dim])
        up = [(i, (i + 1) % count) for i in range(count - 1)]
        down = [(j, i) for i, j in up]
        last = lax.slice_in_dim(shard, length - width, length, axis=dim)
        first = lax.slice_in_dim(shard, 0, width, axis=dim)
        before = lax.ppermute(last, axis, up)
        after = lax.ppermute(first, axis, down)
        shard = jnp.concatenate([before, shard, after], axis=dim)
    return shard


def relative(row_ids, col_ids, sector):
    halfway = G // 2
    row_rot = row_ids % halfway
    row_ref = row_ids // halfway
    col_rot = col_ids % halfway
    col_ref = col_ids // halfway
    sec_rot = sector % halfway
    sec_ref = sector // halfway
    moved_rot = (sec_rot + (1 - 2 * sec_ref) * col_rot) % halfway
    moved_ref = (sec_ref + col_ref) % 2
    inverse_rot = jnp.where(row_ref == 0, (halfway - row_rot) % halfway, row_rot)
    result_rot = (inverse_rot + (1 - 2 * row_ref) * moved_rot) % halfway
    result_ref = (row_ref + moved_ref) % 2
    return result_ref * halfway + result_rot


def kernel_block(kernel, row_ids, col_ids, sector):
    channels = kernel.shape[2]
    tap_count = kernel.shape[1]
    relation = relative(row_ids[:, None], col_ids[None, :], sector).reshape(-1)
    onehot = (relation[:, None] == jnp.arange(G, dtype=jnp.int32)[None, :]).astype(jnp.bfloat16)
    picked = jnp.dot(onehot, kernel.reshape(G, -1), preferred_element_type=jnp.float32)
    picked = picked.reshape(row_ids.shape[0], col_ids.shape[0], tap_count, channels, channels)
    picked = picked.transpose(2, 0, 3, 1, 4)
    return picked.reshape(
        tap_count, row_ids.shape[0] * channels, col_ids.shape[0] * channels
    ).astype(jnp.bfloat16)


def fold_kernel(partial_grad, row_ids, col_ids, sector):
    tap_count = partial_grad.shape[0]
    channels = partial_grad.shape[1] // row_ids.shape[0]
    relation = relative(row_ids[:, None], col_ids[None, :], sector).reshape(-1)
    onehot = (relation[:, None] == jnp.arange(G, dtype=jnp.int32)[None, :]).astype(jnp.float32)
    arranged = partial_grad.reshape(
        tap_count, row_ids.shape[0], channels, col_ids.shape[0], channels
    )
    arranged = arranged.transpose(1, 3, 0, 2, 4).reshape(relation.shape[0], -1)
    folded = jnp.dot(
        onehot.T, arranged, precision=lax.Precision.HIGHEST, preferred_element_type=jnp.float32
    )
    return folded.reshape(G, tap_count, channels, channels)


def place_forward(mixed_taps, height, extent):
    padded = jnp.pad(mixed_taps, ((0, 0), (0, 0), (0, 0), (1, 1)))
    summed = jnp.zeros((mixed_taps.shape[1], height, extent), jnp.float32)
    for tap_index, (row_shift, col_shift) in enumerate(OFFSETS):
        summed = (
            summed
            + padded[tap_index, :, row_shift : row_shift + height, col_shift : col_shift + extent]
        )
    return summed


def place_backward(mixed_taps, height, extent):
    padded = jnp.pad(mixed_taps, ((0, 0), (0, 0), (0, 0), (1, 1)))
    summed = jnp.zeros((mixed_taps.shape[1], height, extent), jnp.float32)
    for tap_index, (row_shift, col_shift) in enumerate(OFFSETS):
        summed = (
            summed
            + padded[
                tap_index,
                :,
                2 - row_shift : 2 - row_shift + height,
                2 - col_shift : 2 - col_shift + extent,
            ]
        )
    return summed


def layer_forward(source, weights_row):
    tap_count, local_width, full_width = weights_row.shape
    height, extent = (source.shape[1], source.shape[2])
    matrix = weights_row.reshape(tap_count * local_width, full_width)
    widened = with_halo(source, (("strip", 1),), 1)
    gathered = lax.all_gather(widened, "orient", axis=0, tiled=True)
    mixed_taps = jnp.dot(
        matrix, gathered.reshape(full_width, -1), preferred_element_type=jnp.float32
    )
    mixed_taps = mixed_taps.reshape(tap_count, local_width, gathered.shape[1], extent)
    center = gathered[:, 1 : height + 1]
    return (place_forward(mixed_taps, height, extent), center)


def rim_rows(gradient):
    return with_halo(gradient, (("strip", 1),), 1)


def weight_grad(cot_rows, center):
    height, extent = (center.shape[1], center.shape[2])
    padded = jnp.pad(cot_rows, ((0, 0), (0, 0), (1, 1)))
    flat_center = center.reshape(center.shape[0], -1)
    pieces = []
    for row_shift, col_shift in OFFSETS:
        window = padded[
            :, 2 - row_shift : 2 - row_shift + height, 2 - col_shift : 2 - col_shift + extent
        ]
        window = window.reshape(cot_rows.shape[0], -1)
        pieces.append(
            lax.dot_general(
                window, flat_center, (((1,), (1,)), ((), ())), preferred_element_type=jnp.float32
            )
        )
    return jnp.stack(pieces, 0)


def shards(inflow_field, kernel_one, kernel_two, turbine_mask, wind_sector, wake_cotangent):
    groups, channels, height, extent = inflow_field.shape
    local_width = groups * channels
    sector = wind_sector[0]
    neutral = jnp.int32(0)
    all_groups = jnp.arange(G, dtype=jnp.int32)
    scale_factor = 1.0 / math.sqrt(G * height * lax.axis_size("strip") * extent)
    first_group = lax.axis_index("orient") * groups
    my_groups = first_group + jnp.arange(groups, dtype=jnp.int32)
    row_one = kernel_block(kernel_one, my_groups, all_groups, sector)
    row_two = kernel_block(kernel_two, my_groups, all_groups, neutral)
    open_cells = (1 - turbine_mask).astype(jnp.float32)
    source = inflow_field.reshape(local_width, height, extent)
    first_pre, first_center = layer_forward(source, row_one)
    sigmoid_one = jax.nn.sigmoid(first_pre)
    hidden = (first_pre * sigmoid_one * open_cells).astype(jnp.bfloat16)
    second_pre, second_center = layer_forward(hidden, row_two)
    wake_out = second_pre.astype(jnp.bfloat16).reshape(groups, channels, height, extent)
    cotangent = wake_cotangent.reshape(local_width, height, extent)
    cot_two = rim_rows(cotangent)
    grad_two = weight_grad(cot_two, second_center)
    rows_turned = row_two.transpose(0, 2, 1)
    mixed_taps = jnp.dot(
        rows_turned.reshape(9 * (local_width * lax.axis_size("orient")), local_width),
        cot_two.reshape(local_width, -1),
        preferred_element_type=jnp.float32,
    )
    mixed_taps = mixed_taps.reshape(9, local_width * lax.axis_size("orient"), height + 2, extent)
    back_grad = lax.psum_scatter(
        place_backward(mixed_taps, height, extent), "orient", scatter_dimension=0, tiled=True
    )
    first_grad = (
        back_grad * open_cells * sigmoid_one * (1.0 + first_pre * (1.0 - sigmoid_one))
    ).astype(jnp.bfloat16)
    cot_one = rim_rows(first_grad)
    grad_one = weight_grad(cot_one, first_center)
    share_one = fold_kernel(grad_one, my_groups, all_groups, sector) * scale_factor
    share_two = fold_kernel(grad_two, my_groups, all_groups, neutral) * scale_factor
    summed_one, summed_two = lax.psum((share_one, share_two), ("orient", "strip"))
    return (wake_out, summed_one, summed_two)


def solution(mesh):
    return jax.shard_map(
        shards,
        mesh=mesh,
        in_specs=(
            P("orient", None, "strip", None),
            P(),
            P(),
            P("strip", None),
            P(),
            P("orient", None, "strip", None),
        ),
        out_specs=(P("orient", None, "strip", None), P(), P()),
        check_vma=False,
    )
```

profile of v0, /device:TPU:2, one launch (start us, length us, event | category | flops | bytes accessed | tf_op | source)
XLA Modules:
  0.0 480.0 jit_solution(5787390711143419611)
XLA Ops:
  8.2 3.8 collective-permute-start
  13.4 4.2 collective-permute-done.1
  19.4 3.8 collective-permute-start.4
  27.4 1.8 convert_element_type.51
  29.9 18.7 %fusion.60 = f32[9,256,10,512]{3,1,2,0:T(8,128)} fusion(bf16[9,16,256]{2,1,0:T(8,128)(2,1)S(1)} %convert_element_type.51, bf16[10,2,8,512]{3,2,1,0:T(8,128)(2,1)S(1)} %get-tuple-element.21), kind=kOutput, calls=%fused_computation.112 | convolution fusion | flops 377487360 | bytes 47423488 | tf_op jit(solution)/shard_map/dot_general | solution.py:153
  48.6 17.5 %fusion.8 = f32[256,8,512]{2,0,1:T(8,128)} fusion(f32[9,256,10,512]{3,1,2,0:T(8,128)} %fusion.60), kind=kLoop, calls=%fused_computation.26 | loop fusion | flops 8388608 | bytes 63963136 | tf_op jit(solution)/shard_map/add | solution.py:84
  68.1 1.7 reshape.552
  69.9 4.4 copy.36
  74.3 2.7 fusion.11
  77.1 61.5 %reduce-scatter.2.cloned.1.call-done = f32[16,8,512]{2,0,1:T(8,128)} async-done(((f32[256,8,512]{2,0,1:T(8,128)}), f32[16,8,512]{2,0,1:T(8,128)}) %reduce-scatter.2.cloned.1.call-update) | async-done | bytes 262160 | tf_op jit(solution)/shard_map/reduce_scatter | solution.py:159
  140.2 3.4 collective-permute-start.2
  145.0 4.2 collective-permute-done.3
  150.0 3.4 reshape.554
  154.9 3.6 collective-permute-start.6
  159.8 2.2 convolution_bitcast_fusion.14
  169.7 1.6 convolution_bitcast_fusion.15
  177.2 1.6 convolution_bitcast_fusion.11
  181.4 8.9 %all-gather.5.cloned.1.call-done = bf16[256,10,512]{2,0,1:T(8,128)(2,1)} async-done(((bf16[16,10,512]{2,0,1:T(8,128)(2,1)}), bf16[256,10,512]{2,0,1:T(8,128)(2,1)}) %all-gather.5.cloned.1.call-update) | async-done | bytes 2621456 | tf_op jit(solution)/shard_map/all_gather | solution.py:100
  190.3 2.4 convolution_bitcast_fusion.10
  210.1 2.6 copy.37
  212.8 2.7 fusion.9
  216.7 253.1 %all-reduce.8.cloned.1.call-done = (f32[32,9,8,8]{0,1,3,2:T(8,128)}, f32[32,9,8,8]{0,1,3,2:T(8,128)}) async-done(((f32[32,9,8,8]{0,1,3,2:T(8,128)}, f32[32,9,8,8]{0,1,3,2:T(8,128)}), (f32[32,9,8,8]{0,1,3,2:T(8,128)}, f32[32,9,8,8]{0,1,3,2:T(8,128)})) %all-reduce.8.cloned.1.call-update) | async-done | bytes 147472 | tf_op jit(solution)/shard_map/psum | solution.py:169
  469.8 1.9 copy.64
  471.6 1.9 copy.65
  (153 shorter events, 51.4 us)
Async XLA Ops:
  7.2 62.7 %all-gather.3.cloned.1.call-start = ((), (), s32[]{:S(2)}) async-start(), calls=%async_computation.1 | async-start | bytes 2785280 | tf_op jit(solution)/shard_map/all_gather | solution.py:100
  8.2 5.3 %collective-permute-start = (bf16[16,1,512]{2,0,1:T(8,128)(2,1)S(1)}, bf16[16,1,512]{2,0,1:T(8,128)(2,1)S(1)}, u32[]{:S(2)}, u32[]{:S(2)}) collective-permute-start(bf16[16,1,512]{2,0,1:T(8,128)(2,1)S(1)} %get-tuple-element.26), channel_id=1, source_target_pairs={{0,1},{1,2},{2,3},{3,4},{4,5},{5,6},{6,7},{7,8},{8,9},{9,10},{10,1... | collective-permute-start | bytes 49160 | tf_op jit(solution)/shard_map/ppermute | solution.py:18
  12.0 5.6 %collective-permute-start.1 = (bf16[16,1,512]{2,0,1:T(8,128)(2,1)S(1)}, bf16[16,1,512]{2,0,1:T(8,128)(2,1)S(1)}, u32[]{:S(2)}, u32[]{:S(2)}) collective-permute-start(bf16[16,1,512]{2,0,1:T(8,128)(2,1)S(1)} %get-tuple-element.27), channel_id=1, source_target_pairs={{1,0},{2,1},{3,2},{4,3},{5,4},{6,5},{7,6},{8,7},{9,8},{10,9},{11,1... | collective-permute-start | bytes 49160 | tf_op jit(solution)/shard_map/ppermute | solution.py:19
  18.3 120.2 %reduce-scatter.2.cloned.1.call-start = ((), (), s32[]{:S(2)}) async-start(), calls=%async_computation.3 | async-start | bytes 4456448 | tf_op jit(solution)/shard_map/reduce_scatter | solution.py:159
  19.4 9.8 %collective-permute-start.4 = (bf16[16,1,512]{2,0,1:T(8,128)(2,1)S(1)}, bf16[16,1,512]{2,0,1:T(8,128)(2,1)S(1)}, u32[]{:S(2)}, u32[]{:S(2)}) collective-permute-start(bf16[16,1,512]{2,0,1:T(8,128)(2,1)S(1)} %get-tuple-element.28), channel_id=1, source_target_pairs={{0,1},{1,2},{2,3},{3,4},{4,5},{5,6},{6,7},{7,8},{8,9},{9,10},{10,1... | collective-permute-start | bytes 49160 | tf_op jit(solution)/shard_map/ppermute | solution.py:18
  23.2 6.7 %collective-permute-start.5 = (bf16[16,1,512]{2,0,1:T(8,128)(2,1)S(1)}, bf16[16,1,512]{2,0,1:T(8,128)(2,1)S(1)}, u32[]{:S(2)}, u32[]{:S(2)}) collective-permute-start(bf16[16,1,512]{2,0,1:T(8,128)(2,1)S(1)} %get-tuple-element.29), channel_id=1, source_target_pairs={{1,0},{2,1},{3,2},{4,3},{5,4},{6,5},{7,6},{8,7},{9,8},{10,9},{11,1... | collective-permute-start | bytes 49160 | tf_op jit(solution)/shard_map/ppermute | solution.py:19
  27.4 21.2 %copy-start.1 = (bf16[9,2,8,32,8]{4,3,2,1,0:T(8,128)(2,1)}, bf16[9,2,8,32,8]{4,3,2,1,0:T(8,128)(2,1)S(1)}, u32[]{:S(2)}) copy-start(bf16[9,2,8,32,8]{4,3,2,1,0:T(8,128)(2,1)S(1)} %copy.32) | copy-start | bytes 221188
  66.1 3.8 copy-start.12
  66.1 124.2 %all-gather.5.cloned.1.call-start = ((), (), s32[]{:S(2)}) async-start(), calls=%async_computation.2 | async-start | bytes 2785280 | tf_op jit(solution)/shard_map/all_gather | solution.py:100
  140.0 22.3 %copy-start.2 = (bf16[256,10,512]{2,0,1:T(8,128)(2,1)S(1)}, bf16[256,10,512]{2,0,1:T(8,128)(2,1)}, u32[]{:S(2)}) copy-start(bf16[256,10,512]{2,0,1:T(8,128)(2,1)} %all-gather.3.cloned.1.call-done) | copy-start | bytes 7864324
  140.2 4.9 %collective-permute-start.2 = (bf16[16,1,512]{2,0,1:T(8,128)(2,1)S(1)}, bf16[16,1,512]{2,0,1:T(8,128)(2,1)S(1)}, u32[]{:S(2)}, u32[]{:S(2)}) collective-permute-start(bf16[16,1,512]{2,0,1:T(8,128)(2,1)S(1)} %get-tuple-element.24), channel_id=1, source_target_pairs={{0,1},{1,2},{2,3},{3,4},{4,5},{5,6},{6,7},{7,8},{8,9},{9,10},{10,1... | collective-permute-start | bytes 49160 | tf_op jit(solution)/shard_map/ppermute | solution.py:18
  143.6 5.6 %collective-permute-start.3 = (bf16[16,1,512]{2,0,1:T(8,128)(2,1)S(1)}, bf16[16,1,512]{2,0,1:T(8,128)(2,1)S(1)}, u32[]{:S(2)}, u32[]{:S(2)}) collective-permute-start(bf16[16,1,512]{2,0,1:T(8,128)(2,1)S(1)} %get-tuple-element.25), channel_id=1, source_target_pairs={{1,0},{2,1},{3,2},{4,3},{5,4},{6,5},{7,6},{8,7},{9,8},{10,9},{11,1... | collective-permute-start | bytes 49160 | tf_op jit(solution)/shard_map/ppermute | solution.py:19
  149.9 319.8 %all-reduce.8.cloned.1.call-start = ((), (), s32[]{:S(2)}) async-start(), calls=%async_computation.4 | async-start | bytes 2097152 | tf_op jit(solution)/shard_map/psum | solution.py:169
  154.9 7.4 %collective-permute-start.6 = (bf16[16,1,512]{2,0,1:T(8,128)(2,1)S(1)}, bf16[16,1,512]{2,0,1:T(8,128)(2,1)S(1)}, u32[]{:S(2)}, u32[]{:S(2)}) collective-permute-start(bf16[16,1,512]{2,0,1:T(8,128)(2,1)S(1)} %get-tuple-element.22), channel_id=1, source_target_pairs={{0,1},{1,2},{2,3},{3,4},{4,5},{5,6},{6,7},{7,8},{8,9},{9,10},{10,1... | collective-permute-start | bytes 49160 | tf_op jit(solution)/shard_map/ppermute | solution.py:18
  158.5 6.0 %collective-permute-start.7 = (bf16[16,1,512]{2,0,1:T(8,128)(2,1)S(1)}, bf16[16,1,512]{2,0,1:T(8,128)(2,1)S(1)}, u32[]{:S(2)}, u32[]{:S(2)}) collective-permute-start(bf16[16,1,512]{2,0,1:T(8,128)(2,1)S(1)} %get-tuple-element.23), channel_id=1, source_target_pairs={{1,0},{2,1},{3,2},{4,3},{5,4},{6,5},{7,6},{8,7},{9,8},{10,9},{11,1... | collective-permute-start | bytes 49160 | tf_op jit(solution)/shard_map/ppermute | solution.py:19
  177.2 1.9 copy-start.8
  177.2 2.0 copy-start.7
  177.2 2.0 copy-start.9
  177.2 2.9 copy-start.14
  190.3 3.3 copy-start
  194.6 1.9 copy-start.3
  200.6 4.4 copy-start.6
  200.9 7.8 %copy-start.13 = (s32[64]{0:T(128)S(1)}, s32[64]{0:T(128)}, u32[]{:S(2)}) copy-start(s32[64]{0:T(128)} %fusion.114) | copy-start | bytes 772
  210.1 2.6 copy-start.5
  (3 other events, 2.2 us)
Sparse Core Ops, SparseCore 0:
  18.5 39.6 all-gather.2
  66.2 72.3 reduce-scatter.1
  150.1 40.1 all-gather.4
  210.2 259.4 all-reduce.7
where the time goes:
time: 481 us; the launch traced here: 480 us
  waiting for transfers between devices  334 us (69%)
  matrix products  48.1 us (10%)
  local copies, waits for them, and re-layouts  39.6 us (8%)
  other arithmetic  23 us (5%)
  starting transfers between devices  20.2 us (4%)
  between operations  15 us (3%)
    psum x1, waiting for transfers between devices, shards(): lax.psum((share_one, share_two), ('orient', 'strip'))  253 us
    reduce_scatter x1, waiting for transfers between devices, shards(): lax.psum_scatter(place_backward(mixed_taps, height, extent), 'orient', sc...  61.5 us
    dot_general x18, matrix products, weight_grad(): lax.dot_general(window, flat_center, (((1,), (1,)), ((), ())), preferred_...  19.6 us
    dot_general x1, matrix products, shards(): jnp.dot(rows_turned.reshape(9 * (local_width * lax.axis_size('orient')),...  18.7 us
    add x1, other arithmetic, place_backward(): summed + padded[tap_index, :, 2 - row_shift:2 - row_shift + height, 2 - c...  17.5 us
    ppermute x4, starting transfers between devices, with_halo(): before = lax.ppermute(last, axis, up)  14.7 us
    unnamed x51, local copies, waits for them, and re-layouts  12.8 us
    ppermute x4, waiting for transfers between devices, with_halo(): after = lax.ppermute(first, axis, down)  10.3 us
  transfers between devices with their start and end apart: 12, of which 9 were waited for; matrix products, arithmetic and copies ran while one was open for 17% of the time, Pallas kernels for 0%

commit v1 on v0

--- a/solution.py
+++ b/solution.py
@@ -97,7 +97,11 @@
     height, extent = (source.shape[1], source.shape[2])
     matrix = weights_row.reshape(tap_count * local_width, full_width)
     widened = with_halo(source, (("strip", 1),), 1)
-    gathered = lax.all_gather(widened, "orient", axis=0, tiled=True)
+    note_quotas = lambda inp, lane_axis: jnp.concatenate(
+        lax.all_to_all(jnp.stack([inp for _ in range(lax.axis_size(lane_axis))]), lane_axis, 0, 0),
+        axis=0,
+    )
+    gathered = note_quotas(widened, "orient")
     mixed_taps = jnp.dot(
         matrix, gathered.reshape(full_width, -1), preferred_element_type=jnp.float32
     )

time: 481 us -> 539 us (1.12); the launches traced: 480 us -> 530 us
  local copies, waits for them, and re-layouts: 39.6 us -> 68.8 us
  starting transfers between devices: 20.2 us -> 38.8 us
    all_to_all x0 -> x2, waiting for transfers between devices: none -> 66.1 us  [layer_forward(): lax.all_to_all(jnp.stack([inp for _ in range(lax.axis_size(lane_axis))]),...]
    reduce_scatter x1, waiting for transfers between devices: 61.5 us -> 1.1 us  [shards(): lax.psum_scatter(place_backward(mixed_taps, height, extent), 'orient', sc...]
    all_to_all x0 -> x2, starting transfers between devices: none -> 14.8 us  [layer_forward(): lax.all_to_all(jnp.stack([inp for _ in range(lax.axis_size(lane_axis))]),...]
    psum x1, waiting for transfers between devices: 253 us -> 263 us  [shards(): lax.psum((share_one, share_two), ('orient', 'strip'))]
    all_to_all x0 -> x4, local copies, waits for them, and re-layouts: none -> 9.7 us  [layer_forward(): lax.all_to_all(jnp.stack([inp for _ in range(lax.axis_size(lane_axis))]),...]
    all_gather x2 -> x0, waiting for transfers between devices: 8.91 us -> none  [layer_forward(): gathered = lax.all_gather(widened, 'orient', axis=0, tiled=True)]
    another operation x38, local copies, waits for them, and re-layouts: 8.5 us -> 16.6 us  [weight_grad(): return jnp.stack(pieces, 0)]
    dot_general x0 -> x2, local copies, waits for them, and re-layouts: none -> 7.39 us  [layer_forward(): jnp.dot(matrix, gathered.reshape(full_width, -1), preferred_element_type=...]
  transfers between devices with their start and end apart: 12 -> 12, of which waited for: 9 -> 7; matrix products, arithmetic and copies ran while one was open for 17% -> 9% of each run, Pallas kernels for 0% -> 0%
where the time goes in v1:
time: 539 us; the launch traced here: 530 us
  waiting for transfers between devices  339 us (63%)
  local copies, waits for them, and re-layouts  68.8 us (13%)
  matrix products  47.6 us (9%)
  starting transfers between devices  38.8 us (7%)
  other arithmetic  19.7 us (4%)
  between operations  15.7 us (3%)
    psum x1, waiting for transfers between devices, shards(): lax.psum((share_one, share_two), ('orient', 'strip'))  263 us
    all_to_all x2, waiting for transfers between devices, layer_forward(): lax.all_to_all(jnp.stack([inp for _ in range(lax.axis_size(lane_axis))]),...  66.1 us
    dot_general x18, matrix products, weight_grad(): lax.dot_general(window, flat_center, (((1,), (1,)), ((), ())), preferred_...  22.1 us
    ppermute x4, starting transfers between devices, with_halo(): before = lax.ppermute(last, axis, up)  18.6 us
    unnamed x58, local copies, waits for them, and re-layouts  18.4 us
    dot_general x1, matrix products, shards(): jnp.dot(rows_turned.reshape(9 * (local_width * lax.axis_size('orient')),...  18.3 us
    add x1, other arithmetic, place_backward(): summed + padded[tap_index, :, 2 - row_shift:2 - row_shift + height, 2 - c...  17.2 us
    another operation x38, local copies, waits for them, and re-layouts, weight_grad(): return jnp.stack(pieces, 0)  16.6 us
  transfers between devices with their start and end apart: 12, of which 7 were waited for; matrix products, arithmetic and copies ran while one was open for 9% of the time, Pallas kernels for 0%

profile of v1, /device:TPU:2, one launch (start us, length us, event | category | flops | bytes accessed | tf_op | source)
XLA Modules:
  0.0 530.0 jit_solution(9401786182140767617)
XLA Ops:
  8.2 3.8 collective-permute-start.4
  18.1 18.3 %fusion.56 = f32[9,256,10,512]{3,1,2,0:T(8,128)} fusion(bf16[9,16,256]{2,1,0:T(8,128)(2,1)S(1)} %convert_element_type.51, bf16[10,2,8,512]{3,2,1,0:T(8,128)(2,1)S(1)} %get-tuple-element.21), kind=kOutput, calls=%fused_computation.108 | convolution fusion | flops 377487360 | bytes 47423488 | tf_op jit(solution)/shard_map/dot_general | solution.py:157
  36.4 17.2 %fusion.8 = f32[256,8,512]{2,0,1:T(8,128)} fusion(f32[9,256,10,512]{3,1,2,0:T(8,128)} %fusion.56), kind=kLoop, calls=%fused_computation.26 | loop fusion | flops 8388608 | bytes 63963136 | tf_op jit(solution)/shard_map/add | solution.py:84
  54.6 4.5 collective-permute-start
  60.6 4.2 collective-permute-done.1
  66.6 6.6 %all-to-all-start = ((bf16[16,16,10,512]{3,1,2,0:T(8,128)(2,1)}), bf16[16,16,10,512]{3,1,2,0:T(8,128)(2,1)S(1)}, u32[]{:S(2)}, u32[]{:S(2)}) async-start(bf16[16,16,10,512]{3,1,2,0:T(8,128)(2,1)} %stack.44), calls=%async_computation | async-start | bytes 5242880 | tf_op jit(solution)/shard_map/all_to_all | solution.py:101
  73.3 2.8 reshape.558
  77.3 2.4 copy.38
  79.6 2.8 reshape.556
  82.8 47.4 %all-to-all-done = bf16[16,16,10,512]{3,1,2,0:T(8,128)(2,1)S(1)} async-done(((bf16[16,16,10,512]{3,1,2,0:T(8,128)(2,1)}), bf16[16,16,10,512]{3,1,2,0:T(8,128)(2,1)S(1)}, u32[]{:S(2)}, u32[]{:S(2)}) %all-to-all-start) | async-done | bytes 2621472 | tf_op jit(solution)/shard_map/all_to_all | solution.py:101
  132.3 4.2 copy.85
  136.5 4.4 copy.43
  148.0 4.7 collective-permute-start.2
  154.0 5.6 %collective-permute-start.6 = (bf16[16,1,512]{2,0,1:T(8,128)(2,1)S(1)}, bf16[16,1,512]{2,0,1:T(8,128)(2,1)S(1)}, u32[]{:S(2)}, u32[]{:S(2)}) collective-permute-start(bf16[16,1,512]{2,0,1:T(8,128)(2,1)S(1)} %get-tuple-element.22), channel_id=1, source_target_pairs={{0,1},{1,2},{2,3},{3,4},{4,5},{5,6},{6,7},{7,8},{8,9},{9,10},{10,1... | collective-permute-start | bytes 49160 | tf_op jit(solution)/shard_map/ppermute | solution.py:18
  161.9 4.5 collective-permute-done.7
  169.8 8.2 %all-to-all-start.1 = ((bf16[16,16,10,512]{3,1,2,0:T(8,128)(2,1)}), bf16[16,16,10,512]{3,1,2,0:T(8,128)(2,1)}, u32[]{:S(2)}, u32[]{:S(2)}) async-start(bf16[16,16,10,512]{3,1,2,0:T(8,128)(2,1)} %stack.45), calls=%async_computation.1 | async-start | bytes 5242880 | tf_op jit(solution)/shard_map/all_to_all | solution.py:101
  191.7 18.6 %all-to-all-done.1 = bf16[16,16,10,512]{3,1,2,0:T(8,128)(2,1)} async-done(((bf16[16,16,10,512]{3,1,2,0:T(8,128)(2,1)}), bf16[16,16,10,512]{3,1,2,0:T(8,128)(2,1)}, u32[]{:S(2)}, u32[]{:S(2)}) %all-to-all-start.1) | async-done | bytes 2621472 | tf_op jit(solution)/shard_map/all_to_all | solution.py:101
  210.3 2.1 copy.61
  222.4 2.2 convolution_bitcast_fusion.2
  234.4 2.2 convolution_bitcast_fusion
  241.2 3.8 copy.44
  245.0 4.4 copy.86
  249.4 3.0 copy.45
  255.9 263.3 %all-reduce.8.cloned.1.call-done = (f32[32,9,8,8]{0,1,3,2:T(8,128)}, f32[32,9,8,8]{0,1,3,2:T(8,128)}) async-done(((f32[32,9,8,8]{0,1,3,2:T(8,128)}, f32[32,9,8,8]{0,1,3,2:T(8,128)}), (f32[32,9,8,8]{0,1,3,2:T(8,128)}, f32[32,9,8,8]{0,1,3,2:T(8,128)})) %all-reduce.8.cloned.1.call-update) | async-done | bytes 147472 | tf_op jit(solution)/shard_map/psum | solution.py:173
  (165 shorter events, 73.1 us)
Async XLA Ops:
  7.2 138.5 %reduce-scatter.2.cloned.1.call-start = ((), (), s32[]{:S(2)}) async-start(), calls=%async_computation.3 | async-start | bytes 4456448 | tf_op jit(solution)/shard_map/reduce_scatter | solution.py:163
  8.2 28.2 %copy-start.4 = (bf16[2,8,8,512]{3,1,0,2:T(8,128)(2,1)}, bf16[2,8,8,512]{3,1,0,2:T(8,128)(2,1)S(1)}, u32[]{:S(2)}) copy-start(bf16[2,8,8,512]{3,1,0,2:T(8,128)(2,1)S(1)} %copy.108) | copy-start | bytes 393220
  8.2 9.8 %collective-permute-start.4 = (bf16[16,1,512]{2,0,1:T(8,128)(2,1)S(1)}, bf16[16,1,512]{2,0,1:T(8,128)(2,1)S(1)}, u32[]{:S(2)}, u32[]{:S(2)}) collective-permute-start(bf16[16,1,512]{2,0,1:T(8,128)(2,1)S(1)} %get-tuple-element.28), channel_id=1, source_target_pairs={{0,1},{1,2},{2,3},{3,4},{4,5},{5,6},{6,7},{7,8},{8,9},{9,10},{10,1... | collective-permute-start | bytes 49160 | tf_op jit(solution)/shard_map/ppermute | solution.py:18
  12.0 6.0 %collective-permute-start.5 = (bf16[16,1,512]{2,0,1:T(8,128)(2,1)S(1)}, bf16[16,1,512]{2,0,1:T(8,128)(2,1)S(1)}, u32[]{:S(2)}, u32[]{:S(2)}) collective-permute-start(bf16[16,1,512]{2,0,1:T(8,128)(2,1)S(1)} %get-tuple-element.29), channel_id=1, source_target_pairs={{1,0},{2,1},{3,2},{4,3},{5,4},{6,5},{7,6},{8,7},{9,8},{10,9},{11,1... | collective-permute-start | bytes 49160 | tf_op jit(solution)/shard_map/ppermute | solution.py:19
  16.2 20.2 %copy-start = (bf16[9,2,8,32,8]{4,3,2,1,0:T(8,128)(2,1)}, bf16[9,2,8,32,8]{4,3,2,1,0:T(8,128)(2,1)S(1)}, u32[]{:S(2)}) copy-start(bf16[9,2,8,32,8]{4,3,2,1,0:T(8,128)(2,1)S(1)} %copy.36) | copy-start | bytes 221188
  18.0 18.4 %copy-start.15 = (bf16[16,1,512]{2,0,1:T(8,128)(2,1)}, bf16[16,1,512]{2,0,1:T(8,128)(2,1)S(1)}, u32[]{:S(2)}) copy-start(bf16[16,1,512]{2,0,1:T(8,128)(2,1)S(1)} %collective-permute-done.4) | copy-start | bytes 49156
  18.0 18.4 %copy-start.16 = (bf16[16,1,512]{2,0,1:T(8,128)(2,1)}, bf16[16,1,512]{2,0,1:T(8,128)(2,1)S(1)}, u32[]{:S(2)}) copy-start(bf16[16,1,512]{2,0,1:T(8,128)(2,1)S(1)} %collective-permute-done.5) | copy-start | bytes 49156
  54.6 6.0 %collective-permute-start = (bf16[16,1,512]{2,0,1:T(8,128)(2,1)S(1)}, bf16[16,1,512]{2,0,1:T(8,128)(2,1)S(1)}, u32[]{:S(2)}, u32[]{:S(2)}) collective-permute-start(bf16[16,1,512]{2,0,1:T(8,128)(2,1)S(1)} %get-tuple-element.26), channel_id=1, source_target_pairs={{0,1},{1,2},{2,3},{3,4},{4,5},{5,6},{6,7},{7,8},{8,9},{9,10},{10,1... | collective-permute-start | bytes 49160 | tf_op jit(solution)/shard_map/ppermute | solution.py:18
  59.1 5.6 %collective-permute-start.1 = (bf16[16,1,512]{2,0,1:T(8,128)(2,1)S(1)}, bf16[16,1,512]{2,0,1:T(8,128)(2,1)S(1)}, u32[]{:S(2)}, u32[]{:S(2)}) collective-permute-start(bf16[16,1,512]{2,0,1:T(8,128)(2,1)S(1)} %get-tuple-element.27), channel_id=1, source_target_pairs={{1,0},{2,1},{3,2},{4,3},{5,4},{6,5},{7,6},{8,7},{9,8},{10,9},{11,1... | collective-permute-start | bytes 49160 | tf_op jit(solution)/shard_map/ppermute | solution.py:19
  66.6 9.5 %copy-start.6 = (bf16[32,9,8,8]{0,3,2,1:T(8,128)(2,1)S(1)}, bf16[32,9,8,8]{0,3,2,1:T(8,128)(2,1)}, u32[]{:S(2)}) copy-start(bf16[32,9,8,8]{0,3,2,1:T(8,128)(2,1)} %param.7) | copy-start | bytes 110596
  66.6 63.6 %all-to-all-start = ((bf16[16,16,10,512]{3,1,2,0:T(8,128)(2,1)}), bf16[16,16,10,512]{3,1,2,0:T(8,128)(2,1)S(1)}, u32[]{:S(2)}, u32[]{:S(2)}) async-start(bf16[16,16,10,512]{3,1,2,0:T(8,128)(2,1)} %stack.44), calls=%async_computation | async-start | bytes 5242880 | tf_op jit(solution)/shard_map/all_to_all | solution.py:101
  73.2 9.5 %copy-start.17 = (s32[8,512]{1,0:T(8,128)S(1)}, s32[8,512]{1,0:T(8,128)}, u32[]{:S(2)}) copy-start(s32[8,512]{1,0:T(8,128)} %param.9) | copy-start | bytes 49156
  145.7 15.2 %copy-start.2 = (bf16[16,16,10,512]{3,1,0,2:T(8,128)(2,1)S(1)}, bf16[16,16,10,512]{3,1,0,2:T(8,128)(2,1)}, u32[]{:S(2)}) copy-start(bf16[16,16,10,512]{3,1,0,2:T(8,128)(2,1)} %copy.49) | copy-start | bytes 7864324
  147.3 19.2 %copy-start.3 = (bf16[16,16,10,512]{3,1,0,2:T(8,128)(2,1)S(1)}, bf16[16,16,10,512]{3,1,0,2:T(8,128)(2,1)}, u32[]{:S(2)}) copy-start(bf16[16,16,10,512]{3,1,0,2:T(8,128)(2,1)} %copy.49) | copy-start | bytes 7864324
  148.0 19.9 %collective-permute-start.2 = (bf16[16,1,512]{2,0,1:T(8,128)(2,1)}, bf16[16,1,512]{2,0,1:T(8,128)(2,1)S(1)}, u32[]{:S(2)}, u32[]{:S(2)}) collective-permute-start(bf16[16,1,512]{2,0,1:T(8,128)(2,1)} %get-tuple-element.24), channel_id=1, source_target_pairs={{0,1},{1,2},{2,3},{3,4},{4,5},{5,6},{6,7},{7,8},{8,9},{9,10},{10,1... | collective-permute-start | bytes 49160 | tf_op jit(solution)/shard_map/ppermute | solution.py:18
  152.7 15.2 %collective-permute-start.3 = (bf16[16,1,512]{2,0,1:T(8,128)(2,1)}, bf16[16,1,512]{2,0,1:T(8,128)(2,1)S(1)}, u32[]{:S(2)}, u32[]{:S(2)}) collective-permute-start(bf16[16,1,512]{2,0,1:T(8,128)(2,1)} %get-tuple-element.25), channel_id=1, source_target_pairs={{1,0},{2,1},{3,2},{4,3},{5,4},{6,5},{7,6},{8,7},{9,8},{10,9},{11,1... | collective-permute-start | bytes 49160 | tf_op jit(solution)/shard_map/ppermute | solution.py:19
  154.0 7.9 %collective-permute-start.6 = (bf16[16,1,512]{2,0,1:T(8,128)(2,1)S(1)}, bf16[16,1,512]{2,0,1:T(8,128)(2,1)S(1)}, u32[]{:S(2)}, u32[]{:S(2)}) collective-permute-start(bf16[16,1,512]{2,0,1:T(8,128)(2,1)S(1)} %get-tuple-element.22), channel_id=1, source_target_pairs={{0,1},{1,2},{2,3},{3,4},{4,5},{5,6},{6,7},{7,8},{8,9},{9,10},{10,1... | collective-permute-start | bytes 49160 | tf_op jit(solution)/shard_map/ppermute | solution.py:18
  159.6 6.8 %collective-permute-start.7 = (bf16[16,1,512]{2,0,1:T(8,128)(2,1)S(1)}, bf16[16,1,512]{2,0,1:T(8,128)(2,1)S(1)}, u32[]{:S(2)}, u32[]{:S(2)}) collective-permute-start(bf16[16,1,512]{2,0,1:T(8,128)(2,1)S(1)} %get-tuple-element.23), channel_id=1, source_target_pairs={{1,0},{2,1},{3,2},{4,3},{5,4},{6,5},{7,6},{8,7},{9,8},{10,9},{11,1... | collective-permute-start | bytes 49160 | tf_op jit(solution)/shard_map/ppermute | solution.py:19
  169.8 40.5 %all-to-all-start.1 = ((bf16[16,16,10,512]{3,1,2,0:T(8,128)(2,1)}), bf16[16,16,10,512]{3,1,2,0:T(8,128)(2,1)}, u32[]{:S(2)}, u32[]{:S(2)}) async-start(bf16[16,16,10,512]{3,1,2,0:T(8,128)(2,1)} %stack.45), calls=%async_computation.1 | async-start | bytes 5242880 | tf_op jit(solution)/shard_map/all_to_all | solution.py:101
  177.9 341.3 %all-reduce.8.cloned.1.call-start = ((), (), s32[]{:S(2)}) async-start(), calls=%async_computation.4 | async-start | bytes 2097152 | tf_op jit(solution)/shard_map/psum | solution.py:173
  234.4 4.2 copy-start.7
  234.4 4.2 copy-start.8
  234.4 4.3 copy-start.9
  234.4 4.3 copy-start.10
  (6 other events, 11.4 us)
Sparse Core Ops, SparseCore 0:
  53.8 91.8 reduce-scatter.1
  253.8 265.3 all-reduce.7
